TPU v7x, 128 devices: a whole 4x4x4 slice. The times are simulated.
128 devices in a mesh: row: 4 (over y), vocab: 32 (over z, x, core).
Axes of the slice: x: 4, y: 4, z: 4, core: 2. Of those that a mesh axis runs over, the one named last changes fastest.
Arguments:
- tokens: bfloat16 [1280, 7168], P(('row', 'vocab')), may hold values from -60 to 60
- norm_gain: float32 [7168], replicated, may hold values from 0.5 to 1.5
- router: bfloat16 [7168, 32], replicated, may hold values from -0.0625 to 0.0625
- routes: int32 [1280, 8], P(('row', 'vocab')), may hold values from 0 to 31, all different within a row; in each aligned block of 10 rows (0 to 9, 10 to 19, ...) at most 3 rows name the same one
- w_gate: bfloat16 [32, 7168, 1024], P('vocab', None, 'row'), may hold values from -0.0625 to 0.0625
- w_up: bfloat16 [32, 7168, 1024], P('vocab', None, 'row'), may hold values from -0.0625 to 0.0625
- w_down: bfloat16 [32, 1024, 7168], P('vocab', 'row'), may hold values from -0.1875 to 0.1875
- head_gain: float32 [7168], replicated, may hold values from 0.5 to 1.5
- head: bfloat16 [65536, 7168], P(('row', 'vocab')), may hold values from -0.18 to 0.18
- draft_logits: bfloat16 [256, 4, 65536], P(None, None, ('row', 'vocab')), may hold values from -18 to 235
- draft_tokens: int32 [256, 4], replicated, may hold values from 0 to 65535
- reject_pos: int32 [256], replicated, may hold values from 0 to 4
Outputs:
- residual: float32 [256, 65536], P(None, ('row', 'vocab'))
- accept: float32 [256, 4], replicated
Inputs may be any that keep to these rules, and one draw needn't show every extreme that they name: `routes`: each row names 8 different experts. Among the rows of one device no expert is named more than 3 times, and some device's rows name some expert exactly 3 times.
All inputs are finite; a program needn't handle non-finite values.
Results may differ from a plain program's by a relative error of at most 0.012.
Values may be sent and summed in bfloat16 or wider, within the bound.
No kernel may reach another device: no remote copies, remote signals or barrier semaphores. Data moves between devices by JAX's collectives and lax.ppermute only.
A program may use at most 256 MiB of HBM per device.

v0:
```python
import jax
import jax.numpy as jnp
from jax import lax
from jax.sharding import PartitionSpec as P

V = 65536
DRAFTS = 4


def rms_norm(values, gain):
    return values * lax.rsqrt(jnp.mean(values * values, axis=-1, keepdims=True) + 1e-06) * gain


def body(
    tokens,
    norm_gain,
    router,
    routes,
    w_gate,
    w_up,
    w_down,
    head_gain,
    head,
    draft_logits,
    draft_tokens,
    reject_pos,
):
    vocab_count = lax.axis_size("vocab")
    rows_dev = tokens.shape[0]
    model_width = tokens.shape[1]
    top_k = routes.shape[1]
    experts = w_gate.shape[0] * vocab_count
    capacity = min(rows_dev, (rows_dev * top_k + experts - 1) // experts)
    ff_part = w_gate.shape[2]
    resid_in = tokens.astype(jnp.float32)
    normed = rms_norm(resid_in, norm_gain).astype(jnp.bfloat16)
    scores = jax.nn.sigmoid(jnp.dot(normed, router, preferred_element_type=jnp.float32))
    member = routes[:, :, None] == jnp.arange(experts, dtype=jnp.int32)[None, None, :]
    chosen = jnp.any(member, axis=1)
    chosen_int = chosen.astype(jnp.int32)
    picked = chosen.astype(jnp.float32) * scores
    weights = 2.5 * picked / jnp.sum(picked, axis=1, keepdims=True)
    earlier = jnp.cumsum(chosen_int, axis=0) - chosen_int
    slot_ids = jnp.arange(capacity, dtype=jnp.int32)[None, :, None]
    selector = ((earlier.T[:, None, :] == slot_ids) & chosen.T[:, None, :]).astype(jnp.float32)
    send_buffer = jnp.einsum(
        "esr,rd->esd", selector.astype(jnp.bfloat16), normed, preferred_element_type=jnp.float32
    ).astype(jnp.bfloat16)
    gate_w = w_gate[0]
    up_w = w_up[0]
    down_w = w_down[0]
    received = lax.all_to_all(send_buffer, "vocab", split_axis=0, concat_axis=0, tiled=True)
    slot_count = received.shape[1]
    shard_piece = lax.all_gather(received, "row", axis=0, tiled=True)
    flat_rows = shard_piece.reshape(-1, model_width)
    gate_out = jnp.dot(flat_rows, gate_w, preferred_element_type=jnp.float32)
    up_out = jnp.dot(flat_rows, up_w, preferred_element_type=jnp.float32)
    hidden_hidden = (jax.nn.silu(gate_out) * up_out).astype(jnp.bfloat16)
    hidden = hidden_hidden.reshape(shard_piece.shape[0], shard_piece.shape[1], ff_part)
    down_out = jnp.dot(hidden.reshape(-1, ff_part), down_w, preferred_element_type=jnp.float32)
    down_out = down_out.astype(jnp.bfloat16).astype(jnp.float32)
    summed = lax.psum_scatter(
        down_out.reshape(received.shape[0] * lax.axis_size("row"), slot_count, model_width).astype(
            jnp.bfloat16
        ),
        "row",
        scatter_dimension=0,
        tiled=True,
    )
    returned = lax.all_to_all(summed, "vocab", split_axis=0, concat_axis=0, tiled=True)
    combine = selector * weights.T[:, None, :]
    moe_sum = jnp.einsum(
        "esr,esd->rd", combine, returned.astype(jnp.float32), precision=lax.Precision.HIGHEST
    )
    mixed_rows = resid_in + moe_sum
    final_normed = rms_norm(mixed_rows, head_gain).astype(jnp.bfloat16)
    local_vocab = head.shape[0]
    logits = lax.dot_general(
        lax.all_gather(final_normed, ("row", "vocab"), axis=0, tiled=True),
        head,
        (((1,), (1,)), ((), ())),
        preferred_element_type=jnp.float32,
    )
    requests = draft_tokens.shape[0]
    slot_total = DRAFTS + 1
    target_logits = logits.reshape(requests, slot_total, local_vocab)
    draft_vals = draft_logits.astype(jnp.float32)
    offset = lax.axis_index(("row", "vocab")) * local_vocab
    local_ids = draft_tokens - offset
    id_match = jnp.arange(local_vocab, dtype=jnp.int32)[None, None, :] == local_ids[:, :, None]
    pick_target = jnp.sum(jnp.where(id_match, target_logits[:, :DRAFTS], 0.0), axis=-1)
    pick_draft = jnp.sum(jnp.where(id_match, draft_vals, 0.0), axis=-1)
    local_top_target = jnp.max(target_logits, axis=-1)
    local_top_draft = jnp.max(draft_vals, axis=-1)
    top_target, top_draft = lax.pmax((local_top_target, local_top_draft), ("row", "vocab"))
    local_sum_target = jnp.sum(jnp.exp(target_logits - top_target[:, :, None]), axis=-1)
    local_sum_draft = jnp.sum(jnp.exp(draft_vals - top_draft[:, :, None]), axis=-1)
    sum_target, sum_draft, pick_t, pick_d = lax.psum(
        (local_sum_target, local_sum_draft, pick_target, pick_draft), ("row", "vocab")
    )
    target = jnp.exp(target_logits - top_target[:, :, None]) / sum_target[:, :, None]
    draft_prob = jnp.exp(draft_vals - top_draft[:, :, None]) / sum_draft[:, :, None]
    log_target = pick_t - top_target[:, :DRAFTS] - jnp.log(sum_target[:, :DRAFTS])
    log_draft = pick_d - top_draft - jnp.log(sum_draft)
    accept = jnp.exp(jnp.minimum(log_target - log_draft, 0.0))
    position = (jnp.arange(slot_total, dtype=jnp.int32)[None, :] == reject_pos[:, None]).astype(
        jnp.float32
    )
    target_at = jnp.sum(position[:, :, None] * target, axis=1)
    draft_at = jnp.sum(position[:, :DRAFTS, None] * draft_prob, axis=1)
    gap_rows = jnp.maximum(target_at - draft_at, 0.0)
    gap_total = lax.psum(jnp.sum(gap_rows, axis=-1), ("row", "vocab"))
    residual = jnp.sqrt(V * gap_rows / gap_total[:, None])
    return (residual, accept)


def solution(mesh):
    placed = (
        P(("row", "vocab"), None),
        P(),
        P(),
        P(("row", "vocab"), None),
        P("vocab", None, "row"),
        P("vocab", None, "row"),
        P("vocab", "row", None),
        P(),
        P(("row", "vocab"), None),
        P(None, None, ("row", "vocab")),
        P(),
        P(),
    )
    return jax.shard_map(
        body,
        mesh=mesh,
        in_specs=placed,
        out_specs=(P(None, ("row", "vocab")), P()),
        check_vma=False,
    )
```

profile of v0, /device:TPU:1, one launch (start us, length us, event | category | flops | bytes accessed | tf_op | source)
XLA Modules:
  0.0 698.3 jit_solution(13152813386539640018)
XLA Ops:
  7.2 0.8 copy.38
  8.2 1.1 fusion.23
  9.3 1.5 convolution_convert_fusion.1
  10.8 1.2 copy.39
  12.0 34.7 %all_to_all.10 = bf16[32,3,7168]{2,1,0:T(4,128)(2,1)S(1)} all-to-all(bf16[32,3,7168]{2,1,0:T(4,128)(2,1)S(1)} %copy.39), channel_id=1, replica_groups=mesh['row'=4,'vocab'=32] {'vocab'}, dimensions={0} | all-to-all | bytes 2752512 | tf_op jit(solution)/shard_map/all_to_all | solution.py:52
  46.7 1.6 copy.40
  48.6 56.5 %all-gather.4.cloned.1.call-done = bf16[128,3,7168]{2,0,1:T(8,128)(2,1)} async-done(((bf16[32,3,7168]{2,0,1:T(8,128)(2,1)}), bf16[128,3,7168]{2,0,1:T(8,128)(2,1)}) %all-gather.4.cloned.1.call-update) | async-done | bytes 5505040 | tf_op jit(solution)/shard_map/all_gather | solution.py:54
  105.1 10.2 %copy.41 = bf16[128,3,7168]{2,1,0:T(4,128)(2,1)} copy(bf16[128,3,7168]{2,0,1:T(8,128)(2,1)} %all-gather.4.cloned.1.call-done) | data formatting | bytes 11010048 | tf_op jit(solution)/shard_map/all_gather | solution.py:54
  115.3 13.0 %reshape.67 = bf16[384,7168]{1,0:T(8,128)(2,1)} reshape(bf16[128,3,7168]{2,1,0:T(4,128)(2,1)} %copy.41) | data formatting | bytes 11010048 | tf_op jit(solution)/shard_map/reshape | solution.py:55
  128.4 5.4 fusion.4
  133.8 0.9 copy-done.12
  134.7 1.6 fusion.17
  136.8 4.0 convolution_convert_fusion
  140.7 12.3 %convert_element_type.57 = bf16[128,3,7168]{2,1,0:T(4,128)(2,1)} reshape(bf16[384,7168]{1,0:T(8,128)(2,1)} %convolution_convert_fusion) | data formatting | bytes 11010048 | tf_op jit(solution)/shard_map/convert_element_type | solution.py:63
  154.9 142.7 %all-reduce.6.cloned.1.call-done = bf16[128,3,7168]{2,1,0:T(4,128)(2,1)} async-done(((bf16[128,3,7168]{2,1,0:T(4,128)(2,1)}), bf16[128,3,7168]{2,1,0:T(4,128)(2,1)}) %all-reduce.6.cloned.1.call-update) | async-done | bytes 5505040
  297.7 3.5 constant_dynamic-slice_fusion
  301.1 8.0 %all-to-all-start.1 = ((bf16[32,3,7168]{2,1,0:T(4,128)(2,1)}), bf16[32,3,7168]{2,1,0:T(4,128)(2,1)S(1)}, u32[]{:S(2)}, u32[]{:S(2)}) async-start(bf16[32,3,7168]{2,1,0:T(4,128)(2,1)} %constant_dynamic-slice_fusion), calls=%async_computation.1 | async-start | bytes 3670016 | tf_op jit(solution)/shard_map/all_to_all | solution.py:70
  309.4 1.4 select_reduce_fusion
  310.8 24.1 %all-to-all-done.1 = bf16[32,3,7168]{2,1,0:T(4,128)(2,1)S(1)} async-done(((bf16[32,3,7168]{2,1,0:T(4,128)(2,1)}), bf16[32,3,7168]{2,1,0:T(4,128)(2,1)S(1)}, u32[]{:S(2)}, u32[]{:S(2)}) %all-to-all-start.1) | async-done | bytes 1376288 | tf_op jit(solution)/shard_map/all_to_all | solution.py:70
  334.9 2.3 multiply_reduce_fusion.1
  339.5 95.4 %all-gather.6.cloned.1.call-done = bf16[128,10,7168]{2,1,0:T(8,128)(2,1)} async-done(((bf16[1,10,7168]{2,1,0:T(8,128)(2,1)}), bf16[128,10,7168]{2,1,0:T(8,128)(2,1)}) %all-gather.6.cloned.1.call-update) | async-done | bytes 18350096 | tf_op jit(solution)/shard_map/all_gather | solution.py:79
  435.0 28.2 %reshape.70 = bf16[1280,7168]{1,0:T(8,128)(2,1)} reshape(bf16[128,10,7168]{2,1,0:T(8,128)(2,1)} %all-gather.6.cloned.1.call-done) | data formatting | bytes 36700160
  463.2 15.7 %fusion.49 = (f32[1280]{0:T(1024)S(1)}, f32[1280,512]{1,0:T(8,128)S(1)}) fusion(bf16[1280,7168]{1,0:T(8,128)(2,1)} %reshape.70, bf16[512,7168]{1,0:T(8,128)(2,1)} %param.20), kind=kOutput, calls=%fused_computation.71 | convolution fusion | flops 9395895296 | bytes 28316672 | tf_op jit(solution)/shard_map/dot_general | solution.py:78
  479.1 65.7 %all-reduce.3 = (f32[256,5]{1,0:T(8,128)S(1)}, f32[256,4]{1,0:T(8,128)S(1)}) all-reduce(f32[256,5]{1,0:T(8,128)S(1)} %reduce_max.26, bf16[256,4]{1,0:T(8,128)(2,1)S(1)} %reduce_max.27), channel_id=1, replica_groups=mesh['row'=4,'vocab'=32] {'row','vocab'}, use_global_device_ids=true, to_apply=%region_7.8 | all-reduce | flops 2304 | bytes 16384 | tf_op jit(solution)/shard_map/pmax | solution.py:95
  545.0 2.1 reshape.68
  547.2 0.9 exponential_reduce_fusion
  548.3 2.4 fusion.8
  550.6 65.5 %all-reduce.2 = (f32[256,5]{1,0:T(8,128)S(1)}, f32[256,4]{1,0:T(8,128)S(1)}) all-reduce(f32[256,5]{1,0:T(8,128)S(1)} %reduce_sum.96, f32[256,4]{1,0:T(8,128)S(1)} %fusion.8), channel_id=1, replica_groups=mesh['row'=4,'vocab'=32] {'row','vocab'}, use_global_device_ids=true, to_apply=%region_9.10 | all-reduce | flops 2304 | bytes 18432 | tf_op jit(solution)/shard_map/psum | solution.py:98
  616.2 3.8 multiply_reduce_fusion
  620.1 5.6 fusion.10
  625.8 64.1 %all-reduce.1 = (f32[256]{0:T(256)S(1)}, f32[256,4]{1,0:T(8,128)S(1)}, f32[256,4]{1,0:T(8,128)S(1)}) all-reduce(f32[256]{0:T(256)S(1)} %fusion.28, f32[256,4]{1,0:T(8,128)} %get-tuple-element.12, f32[256,4]{1,0:T(8,128)S(1)} %get-tuple-element.10), channel_id=1, replica_groups=mesh['row'=4,'vocab'=32] {'row','vocab'}, use_global_device_ids=true, to_apply=%region_17.18 | all-reduce | flops 2304 | bytes 18432 | tf_op jit(solution)/shard_map/psum | solution.py:112
  690.7 1.0 divide_sqrt_fusion
  (52 shorter events, 6.2 us)
Async XLA Ops:
  7.2 302.2 %copy-start = (bf16[7168,32]{0,1:T(8,128)(2,1)S(1)}, bf16[7168,32]{0,1:T(8,128)(2,1)}, u32[]{:S(2)}) copy-start(bf16[7168,32]{0,1:T(8,128)(2,1)} %param.14) | copy-start | bytes 1376260
  7.2 97.9 %all-gather.4.cloned.1.call-start = ((), (), s32[]{:S(2)}) async-start(), calls=%async_computation.2 | async-start | bytes 6881280 | tf_op jit(solution)/shard_map/all_gather | solution.py:54
  48.4 249.3 %all-reduce.6.cloned.1.call-start = ((), (), s32[]{:S(2)}) async-start(), calls=%async_computation.4 | async-start | bytes 14680064
  128.4 5.4 copy-start.5
  128.4 6.3 copy-start.12
  134.7 2.0 copy-start.6
  153.0 0.7 copy-start.13
  154.9 154.4 %copy-start.8 = (f32[7168]{0:T(1024)S(1)}, f32[7168]{0:T(1024)}, u32[]{:S(2)}) copy-start(f32[7168]{0:T(1024)} %param.13) | copy-start | bytes 86020
  301.1 36.1 %copy-start.9 = (f32[7168]{0:T(1024)S(1)}, f32[7168]{0:T(1024)}, u32[]{:S(2)}) copy-start(f32[7168]{0:T(1024)} %param.19) | copy-start | bytes 86020
  301.1 37.0 %copy-start.10 = (s32[256,4]{0,1:T(4,128)S(1)}, s32[256,4]{0,1:T(4,128)}, u32[]{:S(2)}) copy-start(s32[256,4]{0,1:T(4,128)} %param.22) | copy-start | bytes 12292
  301.1 37.8 %copy-start.3 = (bf16[256,4,512]{2,1,0:T(4,128)(2,1)S(1)}, bf16[256,4,512]{2,1,0:T(4,128)(2,1)}, u32[]{:S(2)}) copy-start(bf16[256,4,512]{2,1,0:T(4,128)(2,1)} %param.21) | copy-start | bytes 3145732
  301.1 38.3 %copy-start.11 = (s32[256]{0:T(256)S(1)}, s32[256]{0:T(256)}, u32[]{:S(2)}) copy-start(s32[256]{0:T(256)} %param.23) | copy-start | bytes 3076
  301.1 33.8 %all-to-all-start.1 = ((bf16[32,3,7168]{2,1,0:T(4,128)(2,1)}), bf16[32,3,7168]{2,1,0:T(4,128)(2,1)S(1)}, u32[]{:S(2)}, u32[]{:S(2)}) async-start(bf16[32,3,7168]{2,1,0:T(4,128)(2,1)} %constant_dynamic-slice_fusion), calls=%async_computation.1 | async-start | bytes 3670016 | tf_op jit(solution)/shard_map/all_to_all | solution.py:70
  309.1 125.9 %all-gather.6.cloned.1.call-start = ((), (), s32[]{:S(2)}) async-start(), calls=%async_computation.3 | async-start | bytes 29589504 | tf_op jit(solution)/shard_map/all_gather | solution.py:79
  548.0 72.0 %copy-start.4 = (bf16[256,4,512]{2,1,0:T(4,128)(2,1)S(1)}, bf16[256,4,512]{2,1,0:T(4,128)(2,1)}, u32[]{:S(2)}) copy-start(bf16[256,4,512]{2,1,0:T(4,128)(2,1)} %param.21) | copy-start | bytes 3145732
  548.0 72.0 %copy-start.7 = (s32[256,4]{1,0:T(8,128)S(1)}, s32[256,4]{1,0:T(8,128)}, u32[]{:S(2)}) copy-start(s32[256,4]{1,0:T(8,128)} %copy.43) | copy-start | bytes 12292
  616.2 3.9 copy-start.2
  620.0 71.7 %copy-start.1 = (bf16[7168,32]{0,1:T(8,128)(2,1)S(1)}, bf16[7168,32]{0,1:T(8,128)(2,1)}, u32[]{:S(2)}) copy-start(bf16[7168,32]{0,1:T(8,128)(2,1)} %param.14) | copy-start | bytes 1376260
Sparse Core Ops, SparseCore 0:
  48.5 56.5 all-gather.3
  153.2 144.4 all-reduce.5
  338.2 96.7 all-gather.5
where the time goes:
time: 700 us; the launch traced here: 698 us
  waiting for transfers between devices  319 us (46%)
  blocking collectives  230 us (33%)
  local copies, waits for them, and re-layouts  77.8 us (11%)
  matrix products  31.9 us (5%)
  other arithmetic  16.7 us (2%)
  between operations  14.7 us (2%)
  starting transfers between devices  8.5 us (1%)
    unnamed x4, waiting for transfers between devices  143 us
    all_gather x1, waiting for transfers between devices, body(): lax.all_gather(final_normed, ('row', 'vocab'), axis=0, tiled=True)  95.4 us
    pmax x1, blocking collectives, body(): lax.pmax((local_top_target, local_top_draft), ('row', 'vocab'))  65.7 us
    psum x1, blocking collectives, body(): lax.psum((local_sum_target, local_sum_draft, pick_target, pick_draft), ('...  65.5 us
    psum x1, blocking collectives, body(): gap_total = lax.psum(jnp.sum(gap_rows, axis=-1), ('row', 'vocab'))  64.1 us
    all_gather x1, waiting for transfers between devices, body(): shard_piece = lax.all_gather(received, 'row', axis=0, tiled=True)  56.5 us
    unnamed x33, local copies, waits for them, and re-layouts  35.8 us
    all_to_all x1, blocking collectives, body(): lax.all_to_all(send_buffer, 'vocab', split_axis=0, concat_axis=0, tiled=T...  34.7 us
  transfers between devices with their start and end apart: 4, of which 4 were waited for; matrix products, arithmetic and copies ran while one was open for 0% of the time, Pallas kernels for 0%

commit v1 on v0

--- a/solution.py
+++ b/solution.py
@@ -5,6 +5,11 @@
 
 V = 65536
 DRAFTS = 4
+
+
+def gather_from_all(x, axis, dim):
+    copies = jnp.concatenate([x] * lax.axis_size(axis), axis=dim)
+    return lax.all_to_all(copies, axis, dim, dim, tiled=True)
 
 
 def rms_norm(values, gain):
@@ -51,7 +56,7 @@
     down_w = w_down[0]
     received = lax.all_to_all(send_buffer, "vocab", split_axis=0, concat_axis=0, tiled=True)
     slot_count = received.shape[1]
-    shard_piece = lax.all_gather(received, "row", axis=0, tiled=True)
+    shard_piece = gather_from_all(received, "row", 0)
     flat_rows = shard_piece.reshape(-1, model_width)
     gate_out = jnp.dot(flat_rows, gate_w, preferred_element_type=jnp.float32)
     up_out = jnp.dot(flat_rows, up_w, preferred_element_type=jnp.float32)

time: 700 us -> 720 us (1.029)
  blocking collectives: 230 us -> 316 us
  waiting for transfers between devices: 319 us -> 259 us
  local copies, waits for them, and re-layouts: 77.8 us -> 65.9 us
    all_to_all x0 -> x1, blocking collectives: none -> 85.6 us  [gather_from_all(): return lax.all_to_all(copies, axis, dim, dim, tiled=True)]
    all_gather x1 -> x0, waiting for transfers between devices: 56.5 us -> none  [body(): shard_piece = lax.all_gather(received, 'row', axis=0, tiled=True)]
    all_gather x1 -> x0, local copies, waits for them, and re-layouts: 10.2 us -> none  [body(): shard_piece = lax.all_gather(received, 'row', axis=0, tiled=True)]
    unnamed x4 -> x3, waiting for transfers between devices: 143 us -> 139 us
  transfers between devices with their start and end apart: 4 -> 3, of which waited for: 4 -> 3; matrix products, arithmetic and copies ran while one was open for 0% -> 0% of each run, Pallas kernels for 0% -> 0%
where the time goes in v1:
time: 720 us; the launch traced here: 718 us
  blocking collectives  316 us (44%)
  waiting for transfers between devices  259 us (36%)
  local copies, waits for them, and re-layouts  65.9 us (9%)
  matrix products  31.9 us (4%)
  other arithmetic  22.1 us (3%)
  between operations  15 us (2%)
  starting transfers between devices  8.24 us (1%)
    unnamed x3, waiting for transfers between devices  139 us
    all_gather x1, waiting for transfers between devices, body(): lax.all_gather(final_normed, ('row', 'vocab'), axis=0, tiled=True)  95.4 us
    all_to_all x1, blocking collectives, gather_from_all(): return lax.all_to_all(copies, axis, dim, dim, tiled=True)  85.6 us
    pmax x1, blocking collectives, body(): lax.pmax((local_top_target, local_top_draft), ('row', 'vocab'))  65.7 us
    psum x1, blocking collectives, body(): lax.psum((local_sum_target, local_sum_draft, pick_target, pick_draft), ('...  65.5 us
    psum x1, blocking collectives, body(): gap_total = lax.psum(jnp.sum(gap_rows, axis=-1), ('row', 'vocab'))  64.1 us
    unnamed x33, local copies, waits for them, and re-layouts  35.8 us
    all_to_all x1, blocking collectives, body(): lax.all_to_all(send_buffer, 'vocab', split_axis=0, concat_axis=0, tiled=T...  34.7 us
  transfers between devices with their start and end apart: 3, of which 3 were waited for; matrix products, arithmetic and copies ran while one was open for 0% of the time, Pallas kernels for 0%

profile of v1, /device:TPU:1, one launch (start us, length us, event | category | flops | bytes accessed | tf_op | source)
XLA Modules:
  0.0 717.7 jit_solution(660861492023804209)
XLA Ops:
  7.2 0.8 copy.36
  8.2 1.1 fusion.23
  9.3 1.5 convolution_convert_fusion.1
  10.8 1.2 copy.37
  12.0 34.7 %all_to_all.15 = bf16[32,3,7168]{2,1,0:T(4,128)(2,1)S(1)} all-to-all(bf16[32,3,7168]{2,1,0:T(4,128)(2,1)S(1)} %copy.37), channel_id=1, replica_groups=mesh['row'=4,'vocab'=32] {'vocab'}, dimensions={0} | all-to-all | bytes 2752512 | tf_op jit(solution)/shard_map/all_to_all | solution.py:57
  46.7 5.4 pad_maximum_fusion
  52.2 85.6 %all_to_all.16 = bf16[128,3,7168]{2,1,0:T(4,128)(2,1)} all-to-all(bf16[128,3,7168]{2,1,0:T(4,128)(2,1)S(1)} %pad_maximum_fusion), channel_id=1, replica_groups=mesh['row'=4,'vocab'=32] {'row'}, dimensions={0} | all-to-all | bytes 11010048 | tf_op jit(solution)/shard_map/all_to_all | solution.py:12
  137.8 13.0 %reshape.67 = bf16[384,7168]{1,0:T(8,128)(2,1)} reshape(bf16[128,3,7168]{2,1,0:T(4,128)(2,1)} %all_to_all.16) | data formatting | bytes 11010048 | tf_op jit(solution)/shard_map/reshape | solution.py:60
  150.8 5.4 fusion.4
  156.2 0.9 copy-done.12
  157.1 1.6 fusion.17
  159.2 4.0 convolution_convert_fusion
  163.2 12.3 %convert_element_type.57 = bf16[128,3,7168]{2,1,0:T(4,128)(2,1)} reshape(bf16[384,7168]{1,0:T(8,128)(2,1)} %convolution_convert_fusion) | data formatting | bytes 11010048 | tf_op jit(solution)/shard_map/convert_element_type | solution.py:68
  177.4 139.4 %all-reduce.6.cloned.1.call-done = bf16[128,3,7168]{2,1,0:T(4,128)(2,1)} async-done(((bf16[128,3,7168]{2,1,0:T(4,128)(2,1)}), bf16[128,3,7168]{2,1,0:T(4,128)(2,1)}) %all-reduce.6.cloned.1.call-update) | async-done | bytes 5505040
  316.8 3.5 constant_dynamic-slice_fusion
  320.3 8.0 %all-to-all-start.2 = ((bf16[32,3,7168]{2,1,0:T(4,128)(2,1)}), bf16[32,3,7168]{2,1,0:T(4,128)(2,1)S(1)}, u32[]{:S(2)}, u32[]{:S(2)}) async-start(bf16[32,3,7168]{2,1,0:T(4,128)(2,1)} %constant_dynamic-slice_fusion), calls=%async_computation.2 | async-start | bytes 3670016 | tf_op jit(solution)/shard_map/all_to_all | solution.py:75
  328.5 1.4 select_reduce_fusion
  330.0 24.1 %all-to-all-done.2 = bf16[32,3,7168]{2,1,0:T(4,128)(2,1)S(1)} async-done(((bf16[32,3,7168]{2,1,0:T(4,128)(2,1)}), bf16[32,3,7168]{2,1,0:T(4,128)(2,1)S(1)}, u32[]{:S(2)}, u32[]{:S(2)}) %all-to-all-start.2) | async-done | bytes 1376288 | tf_op jit(solution)/shard_map/all_to_all | solution.py:75
  354.1 2.3 multiply_reduce_fusion.1
  356.4 0.8 fusion.26
  358.7 95.4 %all-gather.3.cloned.1.call-done = bf16[128,10,7168]{2,1,0:T(8,128)(2,1)} async-done(((bf16[1,10,7168]{2,1,0:T(8,128)(2,1)}), bf16[128,10,7168]{2,1,0:T(8,128)(2,1)}) %all-gather.3.cloned.1.call-update) | async-done | bytes 18350096 | tf_op jit(solution)/shard_map/all_gather | solution.py:84
  454.1 28.2 %reshape.70 = bf16[1280,7168]{1,0:T(8,128)(2,1)} reshape(bf16[128,10,7168]{2,1,0:T(8,128)(2,1)} %all-gather.3.cloned.1.call-done) | data formatting | bytes 36700160
  482.4 15.7 %fusion.49 = (f32[1280]{0:T(1024)S(1)}, f32[1280,512]{1,0:T(8,128)S(1)}) fusion(bf16[1280,7168]{1,0:T(8,128)(2,1)} %reshape.70, bf16[512,7168]{1,0:T(8,128)(2,1)} %param.20), kind=kOutput, calls=%fused_computation.72 | convolution fusion | flops 9395895296 | bytes 28316672 | tf_op jit(solution)/shard_map/dot_general | solution.py:83
  498.3 65.7 %all-reduce.3 = (f32[256,5]{1,0:T(8,128)S(1)}, f32[256,4]{1,0:T(8,128)S(1)}) all-reduce(f32[256,5]{1,0:T(8,128)S(1)} %reduce_max.26, bf16[256,4]{1,0:T(8,128)(2,1)S(1)} %reduce_max.27), channel_id=1, replica_groups=mesh['row'=4,'vocab'=32] {'row','vocab'}, use_global_device_ids=true, to_apply=%region_7.8 | all-reduce | flops 2304 | bytes 16384 | tf_op jit(solution)/shard_map/pmax | solution.py:100
  564.2 2.1 reshape.68
  566.3 0.9 exponential_reduce_fusion
  567.4 2.4 fusion.8
  569.8 65.5 %all-reduce.2 = (f32[256,5]{1,0:T(8,128)S(1)}, f32[256,4]{1,0:T(8,128)S(1)}) all-reduce(f32[256,5]{1,0:T(8,128)S(1)} %reduce_sum.96, f32[256,4]{1,0:T(8,128)S(1)} %fusion.8), channel_id=1, replica_groups=mesh['row'=4,'vocab'=32] {'row','vocab'}, use_global_device_ids=true, to_apply=%region_9.10 | all-reduce | flops 2304 | bytes 18432 | tf_op jit(solution)/shard_map/psum | solution.py:103
  635.3 3.8 multiply_reduce_fusion
  639.2 5.6 fusion.10
  644.9 64.1 %all-reduce.1 = (f32[256]{0:T(256)S(1)}, f32[256,4]{1,0:T(8,128)S(1)}, f32[256,4]{1,0:T(8,128)S(1)}) all-reduce(f32[256]{0:T(256)S(1)} %fusion.28, f32[256,4]{1,0:T(8,128)} %get-tuple-element.12, f32[256,4]{1,0:T(8,128)S(1)} %get-tuple-element.10), channel_id=1, replica_groups=mesh['row'=4,'vocab'=32] {'row','vocab'}, use_global_device_ids=true, to_apply=%region_17.18 | all-reduce | flops 2304 | bytes 18432 | tf_op jit(solution)/shard_map/psum | solution.py:117
  709.8 1.0 divide_sqrt_fusion
  (49 shorter events, 5.1 us)
Async XLA Ops:
  7.2 321.3 %copy-start = (bf16[7168,32]{0,1:T(8,128)(2,1)S(1)}, bf16[7168,32]{0,1:T(8,128)(2,1)}, u32[]{:S(2)}) copy-start(bf16[7168,32]{0,1:T(8,128)(2,1)} %param.14) | copy-start | bytes 1376260
  7.2 309.6 %all-reduce.6.cloned.1.call-start = ((), (), s32[]{:S(2)}) async-start(), calls=%async_computation.4 | async-start | bytes 14680064
  150.8 5.4 copy-start.5
  150.8 6.3 copy-start.12
  157.1 2.0 copy-start.6
  175.5 0.7 copy-start.13
  177.4 151.1 %copy-start.8 = (f32[7168]{0:T(1024)S(1)}, f32[7168]{0:T(1024)}, u32[]{:S(2)}) copy-start(f32[7168]{0:T(1024)} %param.13) | copy-start | bytes 86020
  320.3 36.1 %copy-start.9 = (f32[7168]{0:T(1024)S(1)}, f32[7168]{0:T(1024)}, u32[]{:S(2)}) copy-start(f32[7168]{0:T(1024)} %param.19) | copy-start | bytes 86020
  320.3 37.0 %copy-start.10 = (s32[256,4]{0,1:T(4,128)S(1)}, s32[256,4]{0,1:T(4,128)}, u32[]{:S(2)}) copy-start(s32[256,4]{0,1:T(4,128)} %param.22) | copy-start | bytes 12292
  320.3 37.8 %copy-start.3 = (bf16[256,4,512]{2,1,0:T(4,128)(2,1)S(1)}, bf16[256,4,512]{2,1,0:T(4,128)(2,1)}, u32[]{:S(2)}) copy-start(bf16[256,4,512]{2,1,0:T(4,128)(2,1)} %param.21) | copy-start | bytes 3145732
  320.3 38.3 %copy-start.11 = (s32[256]{0:T(256)S(1)}, s32[256]{0:T(256)}, u32[]{:S(2)}) copy-start(s32[256]{0:T(256)} %param.23) | copy-start | bytes 3076
  320.3 33.8 %all-to-all-start.2 = ((bf16[32,3,7168]{2,1,0:T(4,128)(2,1)}), bf16[32,3,7168]{2,1,0:T(4,128)(2,1)S(1)}, u32[]{:S(2)}, u32[]{:S(2)}) async-start(bf16[32,3,7168]{2,1,0:T(4,128)(2,1)} %constant_dynamic-slice_fusion), calls=%async_computation.2 | async-start | bytes 3670016 | tf_op jit(solution)/shard_map/all_to_all | solution.py:75
  328.3 125.9 %all-gather.3.cloned.1.call-start = ((), (), s32[]{:S(2)}) async-start(), calls=%async_computation.3 | async-start | bytes 29589504 | tf_op jit(solution)/shard_map/all_gather | solution.py:84
  567.2 72.0 %copy-start.4 = (bf16[256,4,512]{2,1,0:T(4,128)(2,1)S(1)}, bf16[256,4,512]{2,1,0:T(4,128)(2,1)}, u32[]{:S(2)}) copy-start(bf16[256,4,512]{2,1,0:T(4,128)(2,1)} %param.21) | copy-start | bytes 3145732
  567.2 72.0 %copy-start.7 = (s32[256,4]{1,0:T(8,128)S(1)}, s32[256,4]{1,0:T(8,128)}, u32[]{:S(2)}) copy-start(s32[256,4]{1,0:T(8,128)} %copy.39) | copy-start | bytes 12292
  635.3 3.9 copy-start.2
  639.2 71.7 %copy-start.1 = (bf16[7168,32]{0,1:T(8,128)(2,1)S(1)}, bf16[7168,32]{0,1:T(8,128)(2,1)}, u32[]{:S(2)}) copy-start(bf16[7168,32]{0,1:T(8,128)(2,1)} %param.14) | copy-start | bytes 1376260
Sparse Core Ops, SparseCore 0:
  175.6 141.1 all-reduce.5
  357.4 96.7 all-gather.2
